TPU v7x, 32 devices: a whole 2x2x4 slice. The times are simulated.
32 devices in a mesh: tm: 4 (over y, x), height: 2 (over core), chan: 4 (over z).
Axes of the slice: x: 2, y: 2, z: 4, core: 2. Of those that a mesh axis runs over, the one named last changes fastest.
Arguments:
- features: bfloat16 [384, 8, 8, 160], P('chan', 'tm', 'height'), may hold values from -400 to 400, as said below
- cotangent: bfloat16 [384, 8, 8, 160], P('chan', 'tm', 'height'), may hold values from -6 to 6
- conv_weight: bfloat16 [384, 27, 384], P('chan'), may hold values from -0.0625 to 0.0625
- norm_gain: float32 [384], replicated, may hold values from 0.5 to 1.5
- norm_bias: float32 [384], replicated, may hold values from -3 to 3
Outputs:
- input_grad: bfloat16 [384, 8, 8, 160], P('chan', 'tm', 'height')
- weight_grad: float32 [384, 27, 384], P('chan')
Inputs may be any that keep to these rules, and one draw needn't show every extreme that they name: `features`: bounded activations.
All inputs are finite; a program needn't handle non-finite values.
Results may differ from a plain program's by a relative error of at most 0.003.
Values may be sent and summed in bfloat16 or wider, within the bound.
No kernel may reach another device: no remote copies, remote signals or barrier semaphores. Data moves between devices by JAX's collectives and lax.ppermute only.
A program may use at most 64 MiB of HBM per device.

v0:
```python
import math
import jax
import jax.numpy as jnp
from jax import lax
from jax.sharding import PartitionSpec as P


def from_behind(block, axis, distance):
    devices = range(lax.axis_size(axis))
    route = [(i - distance, i) for i in devices if i - distance in devices]
    return lax.ppermute(block, axis, route)


def with_halo(array, sides, width):
    for axis, dim in sides:
        size, length = (lax.axis_size(axis), array.shape[dim])
        up = [(i, (i + 1) % size) for i in range(size - 1)]
        down = [(j, i) for i, j in up]
        last = lax.slice_in_dim(array, length - width, length, axis=dim)
        first = lax.slice_in_dim(array, 0, width, axis=dim)
        before = lax.ppermute(last, axis, up)
        after = lax.ppermute(first, axis, down)
        array = jnp.concatenate([before, array, after], axis=dim)
    return array


def on_device(features, cotangent, conv_weight, norm_gain, norm_bias):
    chans, frames, rows, cols = features.shape
    whole_x = lax.all_gather(features, "chan", axis=0, tiled=True)
    total = whole_x.shape[0]
    flat_x = whole_x.reshape(total, -1).astype(jnp.float32)
    inv_rms = lax.rsqrt(jnp.mean(flat_x * flat_x, axis=0, keepdims=True) + 1e-06)
    normed = flat_x * inv_rms * norm_gain[:, None] + norm_bias[:, None]
    active = jax.nn.silu(normed).astype(jnp.bfloat16)
    ahead = from_behind(cotangent, "tm", -1)
    longer = jnp.concatenate([cotangent, ahead], axis=1)
    bordered = with_halo(longer, (("height", 2),), 1)
    padded = jnp.pad(bordered, ((0, 0), (0, 0), (0, 0), (1, 1)))
    taps = []
    for kt in range(3):
        for kh in range(3):
            for kw in range(3):
                taps.append(
                    padded[
                        :, 2 - kt : 2 - kt + frames, 2 - kh : 2 - kh + rows, 2 - kw : 2 - kw + cols
                    ]
                )
    stacked = jnp.stack(taps, axis=1).reshape(chans * 27, -1)
    local_sums = lax.dot_general(
        stacked, active, (((1,), (1,)), ((), ())), preferred_element_type=jnp.float32
    )
    positions = frames * lax.axis_size("tm") * rows * lax.axis_size("height") * cols
    summed = lax.psum(local_sums, ("tm", "height"))
    weight_grad = (summed / math.sqrt(positions)).reshape(chans, 27, total)
    sig = jax.nn.sigmoid(normed)
    slope = sig * (1.0 + normed * (1.0 - sig))
    offset = lax.axis_index("chan") * chans
    weight_part = conv_weight.reshape(chans * 27, chans * lax.axis_size("chan"))
    act_grad = lax.psum_scatter(
        lax.dot_general(
            weight_part, stacked, (((0,), (0,)), ((), ())), preferred_element_type=jnp.float32
        ),
        "chan",
        scatter_dimension=0,
        tiled=True,
    )
    own_x = features.reshape(chans, -1).astype(jnp.float32)
    own_slope = lax.dynamic_slice_in_dim(slope, offset, chans, 0)
    own_gain = lax.dynamic_slice_in_dim(norm_gain, offset, chans, 0)
    upstream = act_grad * own_slope * own_gain[:, None]
    dots = lax.psum(jnp.sum(upstream * own_x, axis=0, keepdims=True), "chan")
    own_back = inv_rms * upstream - own_x * inv_rms**3 * dots / total
    result = cotangent.reshape(chans, -1).astype(jnp.float32) + own_back
    return (result.astype(jnp.bfloat16).reshape(features.shape), weight_grad)


def solution(mesh):
    return jax.shard_map(
        on_device,
        mesh=mesh,
        in_specs=(
            P("chan", "tm", "height", None),
            P("chan", "tm", "height", None),
            P("chan", None, None),
            P(),
            P(),
        ),
        out_specs=(P("chan", "tm", "height", None), P("chan", None, None)),
        check_vma=False,
    )
```

profile of v0, /device:TPU:0, one launch (start us, length us, event | category | flops | bytes accessed | tf_op | source)
XLA Modules:
  0.0 245.2 jit_solution(13448478375143645336)
XLA Ops:
  8.0 1.3 collective-permute-start
  9.3 1.3 copy.16
  10.7 31.4 %all_gather.3 = bf16[384,2,4,160]{3,2,1,0:T(4,128)(2,1)S(1)} all-gather(bf16[96,2,4,160]{3,2,1,0:T(4,128)(2,1)S(1)} %copy.16), channel_id=1, replica_groups=mesh['tm'=4,'height'=2,'chan'=4] {'chan'}, dimensions={0}, use_global_device_ids=true | all-gather | bytes 1228800 | tf_op jit(solution)/shard_map/all_gather | solution.py:29
  42.1 1.4 copy.17
  43.9 1.0 constant_dynamic-update-slice_fusion.1
  45.0 1.3 collective-permute-start.1
  46.3 1.3 collective-permute-start.2
  47.6 1.4 multiply_convert_fusion
  50.0 0.8 fusion.53
  52.4 0.8 fusion.51
  54.7 0.8 fusion.49
  55.5 0.8 fusion.24
  59.5 0.8 fusion.45
  61.8 0.8 fusion.42
  64.2 0.8 fusion.40
  68.9 0.8 fusion.34
  71.3 21.1 %copy.18 = bf16[96,27,2,4,160]{4,3,2,1,0:T(4,128)(2,1)} copy(bf16[96,27,2,4,160]{0,4,3,2,1:T(8,128)(2,1)} %fusion.31) | data formatting | bytes 13271040 | tf_op jit(solution)/shard_map/stack | solution.py:48
  92.5 20.4 %reshape.67 = bf16[2592,1280]{1,0:T(8,128)(2,1)} reshape(bf16[96,27,2,4,160]{4,3,2,1,0:T(4,128)(2,1)} %copy.18) | data formatting | bytes 13271040 | tf_op jit(solution)/shard_map/reshape | solution.py:48
  112.8 8.4 %fusion.56 = f32[2592,384]{1,0:T(8,128)} fusion(bf16[2592,1280]{1,0:T(8,128)(2,1)} %reshape.67, bf16[384,1280]{0,1:T(8,128)(2,1)S(1)} %bitcast.128), kind=kOutput, calls=%fused_computation.102 | convolution fusion | flops 2548039680 | bytes 11599872 | tf_op jit(solution)/shard_map/dot_general | solution.py:49
  121.5 2.3 copy.19
  123.8 2.2 reshape.68
  126.0 6.7 %convolution_bitcast_fusion = f32[384,1280]{0,1:T(8,128)S(1)} fusion(bf16[2592,1280]{1,0:T(8,128)(2,1)} %reshape.67, bf16[2592,384]{1,0:T(8,128)(2,1)} %reshape.68), kind=kOutput, calls=%fused_computation.2 | convolution fusion | flops 2548039680 | bytes 10592256 | tf_op jit(solution)/shard_map/dot_general | solution.py:60
  132.7 1.8 copy.21
  134.7 1.8 negate_exponential_fusion
  136.5 66.4 %all-reduce.3.cloned.1.call-done = f32[2592,384]{1,0:T(8,128)} async-done(((f32[2592,384]{1,0:T(8,128)}), f32[2592,384]{1,0:T(8,128)}) %all-reduce.3.cloned.1.call-update) | async-done | bytes 3981328 | tf_op jit(solution)/shard_map/psum | solution.py:53
  202.9 4.4 %broadcast_multiply_fusion = f32[2592,384]{1,0:T(8,128)} fusion(f32[2592,384]{1,0:T(8,128)} %all-reduce.3.cloned.1.call-done), kind=kLoop, calls=%fused_computation.4 | loop fusion | flops 995328 | bytes 7962624 | tf_op jit(solution)/shard_map/div | solution.py:54
  207.3 5.0 %reshape.70 = f32[96,27,384]{2,1,0:T(8,128)} reshape(f32[2592,384]{1,0:T(8,128)} %broadcast_multiply_fusion) | data formatting | bytes 7962624 | tf_op jit(solution)/shard_map/reshape | solution.py:54
  212.3 6.6 %copy.20 = f32[96,27,384]{2,0,1:T(8,128)} copy(f32[96,27,384]{2,1,0:T(8,128)} %reshape.70) | data formatting | bytes 7962624
  218.8 2.1 copy.22
  221.0 2.8 %fusion.13 = (f32[1280]{0:T(1024)S(1)}, f32[96,1280]{0,1:T(8,128)}) fusion(bf16[96,2,4,160]{0,3,2,1:T(8,128)(2,1)S(1)} %copy-done.2, f32[96]{0:T(128)S(1)} %dynamic_slice.7, f32[96,1280]{0,1:T(8,128)} %copy.22, f32[384,1280]{0,1:T(8,128)} %get-tuple-element.13, s32[]{:T(128)S(6)} %select_n.4, f32[384,1280]{0,1:T(8,128)S(1)} %get-tuple-element.12), kind=kLoop, calls=%fused_computation.31 | loop fusion | flops 1350400 | bytes 2217348 | tf_op jit(solution)/shard_map/reduce_sum | solution.py:71
  223.8 11.6 %psum.14 = f32[1280]{0:T(1024)S(1)} all-reduce(f32[1280]{0:T(1024)S(1)} %get-tuple-element.10), channel_id=1, replica_groups=mesh['tm'=4,'height'=2,'chan'=4] {'chan'}, use_global_device_ids=true, to_apply=%region_3.4 | all-reduce | flops 1280 | bytes 10240 | tf_op jit(solution)/shard_map/psum | solution.py:71
  235.4 2.4 fusion.12
  (45 shorter events, 16.5 us)
Async XLA Ops:
  8.0 194.9 %all-reduce.3.cloned.1.call-start = ((), (), s32[]{:S(2)}) async-start(), calls=%async_computation.1 | async-start | bytes 7962624 | tf_op jit(solution)/shard_map/psum | solution.py:53
  8.0 36.9 %collective-permute-start = (bf16[96,2,4,160]{0,3,2,1:T(8,128)(2,1)}, bf16[96,2,4,160]{0,3,2,1:T(8,128)(2,1)S(1)}, u32[]{:S(2)}, u32[]{:S(2)}) collective-permute-start(bf16[96,2,4,160]{0,3,2,1:T(8,128)(2,1)} %param.6), channel_id=1, source_target_pairs={{8,0},{16,8},{24,16},{9,1},{17,9},{25,17},{10,2},{18,10},{26,18},{... | collective-permute-start | bytes 737288 | tf_op jit(solution)/shard_map/ppermute | solution.py:11
  45.0 4.0 %collective-permute-start.1 = (bf16[96,4,1,160]{0,3,2,1:T(8,128)(2,1)S(1)}, bf16[96,4,1,160]{0,3,2,1:T(8,128)(2,1)S(1)}, u32[]{:S(2)}, u32[]{:S(2)}) collective-permute-start(bf16[96,4,1,160]{0,3,2,1:T(8,128)(2,1)S(1)} %get-tuple-element.14), channel_id=1, source_target_pairs={{0,4},{1,5},{2,6},{3,7},{8,12},{9,13},{10,14},{11,15},{16,20},{17,... | collective-permute-start | bytes 368648 | tf_op jit(solution)/shard_map/ppermute | solution.py:21
  46.3 3.3 %collective-permute-start.2 = (bf16[96,4,1,160]{0,3,2,1:T(8,128)(2,1)S(1)}, bf16[96,4,1,160]{0,3,2,1:T(8,128)(2,1)S(1)}, u32[]{:S(2)}, u32[]{:S(2)}) collective-permute-start(bf16[96,4,1,160]{0,3,2,1:T(8,128)(2,1)S(1)} %get-tuple-element.15), channel_id=1, source_target_pairs={{4,0},{5,1},{6,2},{7,3},{12,8},{13,9},{14,10},{15,11},{20,16},{21,... | collective-permute-start | bytes 368648 | tf_op jit(solution)/shard_map/ppermute | solution.py:22
  50.0 17.4 %copy-start = (bf16[96,2,4,160]{0,3,2,1:T(8,128)(2,1)S(1)}, bf16[96,2,4,160]{0,3,2,1:T(8,128)(2,1)}, u32[]{:S(2)}) copy-start(bf16[96,2,4,160]{0,3,2,1:T(8,128)(2,1)} %param.6) | copy-start | bytes 737284
  121.3 97.5 %reduce-scatter.4.cloned.1.call-start = ((), (), s32[]{:S(2)}) async-start(), calls=%async_computation.2 | async-start | bytes 2457600
  126.0 8.6 %copy-start.3 = (f32[384]{0:T(512)S(1)}, f32[384]{0:T(512)}, u32[]{:S(2)}) copy-start(f32[384]{0:T(512)} %param.8) | copy-start | bytes 4612
  126.0 8.7 %copy-start.4 = (f32[384]{0:T(512)S(1)}, f32[384]{0:T(512)}, u32[]{:S(2)}) copy-start(f32[384]{0:T(512)} %param.9) | copy-start | bytes 4612
  207.3 13.7 %copy-start.2 = (bf16[96,2,4,160]{0,3,2,1:T(8,128)(2,1)S(1)}, bf16[96,2,4,160]{0,3,2,1:T(8,128)(2,1)}, u32[]{:S(2)}) copy-start(bf16[96,2,4,160]{0,3,2,1:T(8,128)(2,1)} %param.5) | copy-start | bytes 737284
  207.3 28.1 %copy-start.1 = (bf16[96,2,4,160]{0,3,2,1:T(8,128)(2,1)S(1)}, bf16[96,2,4,160]{0,3,2,1:T(8,128)(2,1)}, u32[]{:S(2)}) copy-start(bf16[96,2,4,160]{0,3,2,1:T(8,128)(2,1)} %param.6) | copy-start | bytes 737284
Sparse Core Ops, SparseCore 0:
  121.4 81.3 all-reduce.2
Sparse Core Ops, SparseCore 1:
  134.6 44.6 reduce-scatter.3
where the time goes:
time: 247 us; the launch traced here: 245 us
  local copies, waits for them, and re-layouts  82 us (33%)
  waiting for transfers between devices  67 us (27%)
  blocking collectives  43 us (17%)
  other arithmetic  18.3 us (7%)
  between operations  15.6 us (6%)
  matrix products  15.1 us (6%)
  starting transfers between devices  4.15 us (2%)
    psum x1, waiting for transfers between devices, on_device(): summed = lax.psum(local_sums, ('tm', 'height'))  66.4 us
    all_gather x1, blocking collectives, on_device(): whole_x = lax.all_gather(features, 'chan', axis=0, tiled=True)  31.4 us
    unnamed x36, local copies, waits for them, and re-layouts  30.9 us
    another operation x2, local copies, waits for them, and re-layouts, on_device(): stacked = jnp.stack(taps, axis=1).reshape(chans * 27, -1)  21.9 us
    reshape x1, local copies, waits for them, and re-layouts, on_device(): stacked = jnp.stack(taps, axis=1).reshape(chans * 27, -1)  20.4 us
    psum x1, blocking collectives, on_device(): dots = lax.psum(jnp.sum(upstream * own_x, axis=0, keepdims=True), 'chan')  11.6 us
    dot_general x1, matrix products, on_device(): lax.dot_general(stacked, active, (((1,), (1,)), ((), ())), preferred_elem...  8.42 us
    dot_general x1, matrix products, on_device(): lax.dot_general(weight_part, stacked, (((0,), (0,)), ((), ())), preferred...  6.67 us
  transfers between devices with their start and end apart: 5, of which 2 were waited for; matrix products, arithmetic and copies ran while one was open for 15% of the time, Pallas kernels for 0%

commit v1 on v0

--- a/solution.py
+++ b/solution.py
@@ -50,7 +50,8 @@
         stacked, active, (((1,), (1,)), ((), ())), preferred_element_type=jnp.float32
     )
     positions = frames * lax.axis_size("tm") * rows * lax.axis_size("height") * cols
-    summed = lax.psum(local_sums, ("tm", "height"))
+    shards = lax.all_gather(local_sums, ("tm", "height"))
+    summed = jnp.sum(shards, axis=0)
     weight_grad = (summed / math.sqrt(positions)).reshape(chans, 27, total)
     sig = jax.nn.sigmoid(normed)
     slope = sig * (1.0 + normed * (1.0 - sig))

time: 247 us -> 368 us (1.49)
  waiting for transfers between devices: 67 us -> 145 us
  blocking collectives: 43 us -> 66.1 us
  other arithmetic: 18.3 us -> 32.5 us
    all_gather x0 -> x1, waiting for transfers between devices: none -> 135 us  [on_device(): shards = lax.all_gather(local_sums, ('tm', 'height'))]
    psum x1 -> x0, waiting for transfers between devices: 66.4 us -> none  [on_device(): summed = lax.psum(local_sums, ('tm', 'height'))]
    all_gather x1, blocking collectives: 31.4 us -> 53.5 us  [on_device(): whole_x = lax.all_gather(features, 'chan', axis=0, tiled=True)]
    reduce_sum x0 -> x1, other arithmetic: none -> 13.9 us  [on_device(): summed = jnp.sum(shards, axis=0)]
    ppermute x1, waiting for transfers between devices: 0.01 us -> 10.5 us  [from_behind(): return lax.ppermute(block, axis, route)]
    reshape x1 -> x0, local copies, waits for them, and re-layouts: 4.98 us -> none  [on_device(): weight_grad = (summed / math.sqrt(positions)).reshape(chans, 27, total)]
    div x0 -> x1, local copies, waits for them, and re-layouts: none -> 4.92 us  [on_device(): weight_grad = (summed / math.sqrt(positions)).reshape(chans, 27, total)]
    unnamed x36 -> x42, local copies, waits for them, and re-layouts: 30.9 us -> 32.6 us
  transfers between devices with their start and end apart: 5 -> 5, of which waited for: 2 -> 2; matrix products, arithmetic and copies ran while one was open for 15% -> 7% of each run, Pallas kernels for 0% -> 0%
where the time goes in v1:
time: 368 us; the launch traced here: 366 us
  waiting for transfers between devices  145 us (39%)
  local copies, waits for them, and re-layouts  84.4 us (23%)
  blocking collectives  66.1 us (18%)
  other arithmetic  32.5 us (9%)
  matrix products  16.6 us (5%)
  between operations  15.6 us (4%)
  starting transfers between devices  5.7 us (2%)
    all_gather x1, waiting for transfers between devices, on_device(): shards = lax.all_gather(local_sums, ('tm', 'height'))  135 us
    all_gather x1, blocking collectives, on_device(): whole_x = lax.all_gather(features, 'chan', axis=0, tiled=True)  53.5 us
    unnamed x42, local copies, waits for them, and re-layouts  32.6 us
    another operation x2, local copies, waits for them, and re-layouts, on_device(): stacked = jnp.stack(taps, axis=1).reshape(chans * 27, -1)  21.8 us
    reshape x1, local copies, waits for them, and re-layouts, on_device(): stacked = jnp.stack(taps, axis=1).reshape(chans * 27, -1)  20.5 us
    reduce_sum x1, other arithmetic, on_device(): summed = jnp.sum(shards, axis=0)  13.9 us
    psum x1, blocking collectives, on_device(): dots = lax.psum(jnp.sum(upstream * own_x, axis=0, keepdims=True), 'chan')  12.6 us
    ppermute x1, waiting for transfers between devices, from_behind(): return lax.ppermute(block, axis, route)  10.5 us
  transfers between devices with their start and end apart: 5, of which 2 were waited for; matrix products, arithmetic and copies ran while one was open for 7% of the time, Pallas kernels for 0%

profile of v1, /device:TPU:0, one launch (start us, length us, event | category | flops | bytes accessed | tf_op | source)
XLA Modules:
  0.0 366.3 jit_solution(4276430643013541657)
XLA Ops:
  8.0 1.3 collective-permute-start
  9.3 1.0 constant_dynamic-update-slice_fusion.1
  10.3 10.5 %collective-permute-done = bf16[96,2,4,160]{0,3,2,1:T(8,128)(2,1)S(1)} collective-permute-done((bf16[96,2,4,160]{0,3,2,1:T(8,128)(2,1)}, bf16[96,2,4,160]{0,3,2,1:T(8,128)(2,1)S(1)}, u32[]{:S(2)}, u32[]{:S(2)}) %collective-permute-start) | collective-permute-done | bytes 245792 | tf_op jit(solution)/shard_map/ppermute | solution.py:11
  21.6 1.3 collective-permute-start.2
  22.9 3.0 collective-permute-start.1
  26.0 2.3 copy.18
  28.3 2.1 reshape.69
  31.4 0.8 fusion.53
  32.3 1.7 fusion.30
  35.5 1.7 bitcast_dynamic-update-slice_fusion.1
  38.0 0.8 fusion.49
  41.2 1.7 fusion.27
  43.6 0.8 fusion.45
  45.9 0.8 fusion.42
  48.3 0.8 fusion.40
  55.3 21.1 %copy.17 = bf16[96,27,2,4,160]{4,3,2,1,0:T(4,128)(2,1)} copy(bf16[96,27,2,4,160]{0,4,3,2,1:T(8,128)(2,1)} %fusion.31) | data formatting | bytes 13271040 | tf_op jit(solution)/shard_map/stack | solution.py:48
  76.4 20.5 %reshape.68 = bf16[2592,1280]{1,0:T(8,128)(2,1)} reshape(bf16[96,27,2,4,160]{4,3,2,1,0:T(4,128)(2,1)} %copy.17) | data formatting | bytes 13271040 | tf_op jit(solution)/shard_map/reshape | solution.py:48
  97.0 8.1 %convolution_bitcast_fusion = f32[384,1280]{0,1:T(8,128)} fusion(bf16[2592,1280]{1,0:T(8,128)(2,1)} %reshape.68, bf16[2592,384]{1,0:T(8,128)(2,1)S(1)} %copy-done.4), kind=kOutput, calls=%fused_computation.2 | convolution fusion | flops 2548039680 | bytes 10592256 | tf_op jit(solution)/shard_map/dot_general | solution.py:61
  105.0 2.9 copy.20
  108.4 53.5 %all_gather.9 = bf16[384,2,4,160]{3,2,1,0:T(4,128)(2,1)S(1)} all-gather(bf16[96,2,4,160]{3,2,1,0:T(4,128)(2,1)S(1)} %copy.15), channel_id=1, replica_groups=mesh['tm'=4,'height'=2,'chan'=4] {'chan'}, dimensions={0}, use_global_device_ids=true | all-gather | bytes 1228800 | tf_op jit(solution)/shard_map/all_gather | solution.py:29
  161.9 1.4 copy.16
  164.5 8.5 %fusion.56 = f32[2592,384]{1,0:T(8,128)} fusion(bf16[2592,1280]{1,0:T(8,128)(2,1)} %reshape.68, bf16[384,1280]{0,1:T(8,128)(2,1)S(1)} %bitcast.130), kind=kOutput, calls=%fused_computation.102 | convolution fusion | flops 2548039680 | bytes 11599872 | tf_op jit(solution)/shard_map/dot_general | solution.py:49
  173.1 1.7 negate_exponential_fusion
  174.9 2.1 copy.21
  177.0 2.2 fusion.13
  179.3 12.6 %psum.7 = f32[1280]{0:T(1024)S(1)} all-reduce(f32[1280]{0:T(1024)S(1)} %get-tuple-element.8), channel_id=1, replica_groups=mesh['tm'=4,'height'=2,'chan'=4] {'chan'}, use_global_device_ids=true, to_apply=%region_3.4 | all-reduce | flops 1280 | bytes 10240 | tf_op jit(solution)/shard_map/psum | solution.py:72
  191.8 2.3 fusion.12
  194.1 135.0 %all-gather.3.cloned.1.call-done = f32[20736,384]{1,0:T(8,128)} async-done(((f32[2592,384]{1,0:T(8,128)}), f32[20736,384]{1,0:T(8,128)}) %all-gather.3.cloned.1.call-update) | async-done | bytes 31850512 | tf_op jit(solution)/shard_map/all_gather | solution.py:53
  329.1 13.9 %reduce_sum.29 = f32[2592,384]{1,0:T(8,128)} reduce(f32[8,2592,384]{2,1,0:T(8,128)} %bitcast.129, f32[]{:T(128)} %constant.10.clone.1), dimensions={0}, to_apply=%region_4.5 | reduce | flops 6967296 | bytes 35831812 | tf_op jit(solution)/shard_map/reduce_sum | solution.py:54
  342.9 4.4 %broadcast_multiply_fusion = f32[2592,384]{1,0:T(8,128)} fusion(f32[2592,384]{1,0:T(8,128)} %reduce_sum.29), kind=kLoop, calls=%fused_computation.4 | loop fusion | flops 995328 | bytes 7962624 | tf_op jit(solution)/shard_map/div | solution.py:55
  347.4 4.9 %div.36 = f32[96,27,384]{2,1,0:T(8,128)} reshape(f32[2592,384]{1,0:T(8,128)} %broadcast_multiply_fusion) | data formatting | bytes 7962624 | tf_op jit(solution)/shard_map/div | solution.py:55
  352.3 6.6 %copy.19 = f32[96,27,384]{2,0,1:T(8,128)} copy(f32[96,27,384]{2,1,0:T(8,128)} %div.36) | data formatting | bytes 7962624
  (52 shorter events, 18.2 us)
Async XLA Ops:
  8.0 166.9 %reduce-scatter.4.cloned.1.call-start = ((), (), s32[]{:S(2)}) async-start(), calls=%async_computation.2 | async-start | bytes 2457600
  8.0 12.8 %collective-permute-start = (bf16[96,2,4,160]{0,3,2,1:T(8,128)(2,1)}, bf16[96,2,4,160]{0,3,2,1:T(8,128)(2,1)S(1)}, u32[]{:S(2)}, u32[]{:S(2)}) collective-permute-start(bf16[96,2,4,160]{0,3,2,1:T(8,128)(2,1)} %param.6), channel_id=1, source_target_pairs={{8,0},{16,8},{24,16},{9,1},{17,9},{25,17},{10,2},{18,10},{26,18},{... | collective-permute-start | bytes 737288 | tf_op jit(solution)/shard_map/ppermute | solution.py:11
  20.8 2.1 copy-start.5
  21.6 8.8 %collective-permute-start.2 = (bf16[96,4,1,160]{0,3,2,1:T(8,128)(2,1)}, bf16[96,4,1,160]{0,3,2,1:T(8,128)(2,1)S(1)}, u32[]{:S(2)}, u32[]{:S(2)}) collective-permute-start(bf16[96,4,1,160]{0,3,2,1:T(8,128)(2,1)} %get-tuple-element.13), channel_id=1, source_target_pairs={{4,0},{5,1},{6,2},{7,3},{12,8},{13,9},{14,10},{15,11},{20,16},{21,... | collective-permute-start | bytes 368648 | tf_op jit(solution)/shard_map/ppermute | solution.py:22
  22.9 7.5 %collective-permute-start.1 = (bf16[96,4,1,160]{0,3,2,1:T(8,128)(2,1)}, bf16[96,4,1,160]{0,3,2,1:T(8,128)(2,1)S(1)}, u32[]{:S(2)}, u32[]{:S(2)}) collective-permute-start(bf16[96,4,1,160]{0,3,2,1:T(8,128)(2,1)} %get-tuple-element.12), channel_id=1, source_target_pairs={{0,4},{1,5},{2,6},{3,7},{8,12},{9,13},{10,14},{11,15},{16,20},{17,... | collective-permute-start | bytes 368648 | tf_op jit(solution)/shard_map/ppermute | solution.py:21
  30.4 0.7 copy-start.2
  31.4 17.7 %copy-start.3 = (bf16[96,4,1,160]{0,3,2,1:T(8,128)(2,1)S(1)}, bf16[96,4,1,160]{0,3,2,1:T(8,128)(2,1)}, u32[]{:S(2)}) copy-start(bf16[96,4,1,160]{0,3,2,1:T(8,128)(2,1)} %copy-done.2) | copy-start | bytes 368644
  31.4 20.0 %copy-start = (bf16[96,2,4,160]{0,3,2,1:T(8,128)(2,1)S(1)}, bf16[96,2,4,160]{0,3,2,1:T(8,128)(2,1)}, u32[]{:S(2)}) copy-start(bf16[96,2,4,160]{0,3,2,1:T(8,128)(2,1)} %param.6) | copy-start | bytes 737284
  76.4 20.5 %copy-start.4 = (bf16[2592,384]{1,0:T(8,128)(2,1)S(1)}, bf16[2592,384]{1,0:T(8,128)(2,1)}, u32[]{:S(2)}) copy-start(bf16[2592,384]{1,0:T(8,128)(2,1)} %reshape.69) | copy-start | bytes 5971972
  97.0 11.1 %copy-start.1 = (bf16[96,2,4,160]{0,3,2,1:T(8,128)(2,1)S(1)}, bf16[96,2,4,160]{0,3,2,1:T(8,128)(2,1)}, u32[]{:S(2)}) copy-start(bf16[96,2,4,160]{0,3,2,1:T(8,128)(2,1)} %param.5) | copy-start | bytes 737284
  105.0 58.7 %copy-start.6 = (f32[384]{0:T(512)S(1)}, f32[384]{0:T(512)}, u32[]{:S(2)}) copy-start(f32[384]{0:T(512)} %param.8) | copy-start | bytes 4612
  105.0 58.7 %copy-start.7 = (f32[384]{0:T(512)S(1)}, f32[384]{0:T(512)}, u32[]{:S(2)}) copy-start(f32[384]{0:T(512)} %param.9) | copy-start | bytes 4612
  108.0 221.1 %all-gather.3.cloned.1.call-start = ((), (), s32[]{:S(2)}) async-start(), calls=%async_computation.1 | async-start | bytes 35831808 | tf_op jit(solution)/shard_map/all_gather | solution.py:53
Sparse Core Ops, SparseCore 0:
  108.1 62.4 reduce-scatter.3
Sparse Core Ops, SparseCore 1:
  173.1 156.0 all-gather.2
